TPU v7x, 32 devices: a whole 2x2x4 slice. The times are simulated.
32 devices in a mesh: groups: 2 (over x), blk: 16 (over z, y, core).
Axes of the slice: x: 2, y: 2, z: 4, core: 2. Of those that a mesh axis runs over, the one named last changes fastest.
Arguments:
- paths: bfloat16 [4096, 512], P(('groups', 'blk')), parts along dimension 0, may hold values from -6 to 6
- deltas: bfloat16 [4096, 512], P(('groups', 'blk')), parts along dimension 0, may hold values from -6 to 6
- payoffs: bfloat16 [4096], P(('groups', 'blk')), parts along dimension 0, may hold values from -6 to 6
- counts: int32 [32, 16], P('groups'), parts along dimension 0, may hold values from 0 to 8, as said below
- w_first: bfloat16 [1024, 1024], P(('groups', 'blk')), parts along dimension 0, may hold values from -0.25 to 0.25
- w_second: bfloat16 [2048, 1024], P(('groups', 'blk')), parts along dimension 0, may hold values from -0.1875 to 0.1875
- w_out: bfloat16 [2048], P('groups'), parts along dimension 0, may hold values from -0.1875 to 0.1875
- mom_first: float32 [1024, 1024], P(('groups', 'blk')), parts along dimension 0, may hold values from -6 to 6
- mom_second: float32 [2048, 1024], P(('groups', 'blk')), parts along dimension 0, may hold values from -6 to 6
- mom_out: float32 [2048], P('groups'), parts along dimension 0, may hold values from -6 to 6
Outputs:
- new_first: float32 [1024, 1024], P(('groups', 'blk')), parts along dimension 0
- new_second: float32 [2048, 1024], P(('groups', 'blk')), parts along dimension 0
- new_out: float32 [2048], P('groups'), parts along dimension 0
There are 2 independent parts, one for each index of `groups`. A program takes and returns all parts, laid end to end along the dimension named above; each array names one. Nothing has to cross between parts.
Inputs may be any that keep to these rules, and one draw needn't show every extreme that they name: Source s hands its valid paths, slot 0 onward, to the trainers in order: counts[s, d] of them to trainer d. Every trainer receives 64 paths or fewer in all, and one receives exactly 64; one source hands 8 to every trainer.
All inputs are finite; a program needn't handle non-finite values.
Results may differ from a plain program's by a relative error of at most 0.00035.
The roundings to bfloat16 on the way count: a program that leaves them out, or rounds other values in their place, can miss the bound.
Values may be sent and summed in bfloat16 or wider, within the bound.
No kernel may reach another device: no remote copies, remote signals or barrier semaphores. Data moves between devices by JAX's collectives and lax.ppermute only.
A program may use at most 64 MiB of HBM per device.

v0:
```python
import jax
import jax.numpy as jnp
from jax import lax
from jax.sharding import PartitionSpec as P


def rows_product(left, right):
    return lax.dot_general(
        left, right, (((0,), (0,)), ((), ())), preferred_element_type=jnp.float32
    )


def twin_terms(x_rows, z_rows, y_rows, mask, w_one, w_two, w_three):
    w_outf = w_three.astype(jnp.float32)
    a_one = jnp.dot(x_rows, w_one, preferred_element_type=jnp.float32)
    s_one = jax.nn.sigmoid(a_one)
    h_one = jax.nn.softplus(a_one).astype(jnp.bfloat16)
    a_two = jnp.dot(h_one, w_two, preferred_element_type=jnp.float32)
    s_two = jax.nn.sigmoid(a_two)
    h_two = jax.nn.softplus(a_two)
    value = jnp.sum(h_two * w_outf[None, :], axis=1)
    g_two = (s_two * w_outf[None, :]).astype(jnp.bfloat16)
    c_one = lax.dot_general(
        g_two, w_two, (((1,), (1,)), ((), ())), preferred_element_type=jnp.float32
    )
    g_one = (c_one * s_one).astype(jnp.bfloat16)
    slope = lax.dot_general(
        g_one, w_one, (((1,), (1,)), ((), ())), preferred_element_type=jnp.float32
    )
    e_value = 2.0 * mask * (value - y_rows.astype(jnp.float32))
    e_slope = (2.0 * mask[:, None] * (slope - z_rows.astype(jnp.float32))).astype(jnp.bfloat16)
    e_gone = jnp.dot(e_slope, w_one, preferred_element_type=jnp.float32)
    e_cone = (e_gone * s_one).astype(jnp.bfloat16)
    e_sone = e_gone * c_one
    e_gtwo = jnp.dot(e_cone, w_two, preferred_element_type=jnp.float32)
    grad_three = jnp.sum(e_gtwo * s_two + e_value[:, None] * h_two, axis=0)
    e_atwo = (
        e_gtwo * w_outf[None, :] * s_two * (1.0 - s_two)
        + e_value[:, None] * w_outf[None, :] * s_two
    ).astype(jnp.bfloat16)
    e_hone = lax.dot_general(
        e_atwo, w_two, (((1,), (1,)), ((), ())), preferred_element_type=jnp.float32
    )
    e_aone = (e_sone * s_one * (1.0 - s_one) + e_hone * s_one).astype(jnp.bfloat16)
    return (e_slope, g_one, e_aone, e_cone, g_two, h_one, e_atwo, grad_three)


def normalized(grad):
    return grad / jnp.sqrt(jnp.mean(grad * grad, axis=-1, keepdims=True) + 1e-06)


def per_device(
    paths, deltas, payoffs, counts, w_first, w_second, w_out, mom_first, mom_second, mom_out
):
    position = lax.axis_index("blk")
    rows_dev = paths.shape[0]
    w_one, w_two = (
        lax.all_gather(w_first, "blk", axis=0, tiled=True),
        lax.all_gather(w_second, "blk", axis=0, tiled=True),
    )
    sending = lax.dynamic_index_in_dim(counts, position, 0, keepdims=False)
    x_rows, z_rows, y_rows = (paths, deltas, payoffs)
    total = jnp.sum(sending)
    mask = (jnp.arange(rows_dev, dtype=jnp.int32) < total).astype(jnp.float32)
    e_slope, g_one, e_aone, e_cone, g_two, h_one, e_atwo, grad_three = twin_terms(
        x_rows, z_rows, y_rows, mask, w_one, w_two, w_out
    )
    grad_one = lax.psum_scatter(
        rows_product(x_rows, e_aone) + rows_product(e_slope, g_one),
        "blk",
        scatter_dimension=0,
        tiled=True,
    )
    grad_two = lax.psum_scatter(
        rows_product(e_cone, g_two) + rows_product(h_one, e_atwo),
        "blk",
        scatter_dimension=0,
        tiled=True,
    )
    grad_out = lax.psum(grad_three, "blk")
    new_first = 0.8 * mom_first + 0.2 * normalized(grad_one)
    new_second = 0.8 * mom_second + 0.2 * normalized(grad_two)
    new_out = 0.8 * mom_out + 0.2 * normalized(grad_out)
    return (new_first, new_second, new_out)


def solution(mesh):
    in_specs = (
        P(("groups", "blk"), None),
        P(("groups", "blk"), None),
        P(("groups", "blk")),
        P("groups", None),
        P(("groups", "blk"), None),
        P(("groups", "blk"), None),
        P("groups"),
        P(("groups", "blk"), None),
        P(("groups", "blk"), None),
        P("groups"),
    )
    out_specs = (P(("groups", "blk"), None), P(("groups", "blk"), None), P("groups"))
    return jax.shard_map(
        per_device, mesh=mesh, in_specs=in_specs, out_specs=out_specs, check_vma=False
    )
```

profile of v0, /device:TPU:0, one launch (start us, length us, event | category | flops | bytes accessed | tf_op | source)
XLA Modules:
  0.0 254.4 jit_solution(2150444523015975469)
XLA Ops:
  8.0 0.7 all-gather.5.cloned.1.call-update
  8.7 0.7 convert_element_type.33
  9.4 1.3 dynamic-slice_reduce_fusion
  11.4 39.5 %all-gather.3.cloned.1.call-done = bf16[512,1024]{1,0:T(8,128)(2,1)} async-done(((bf16[32,1024]{1,0:T(8,128)(2,1)}), bf16[512,1024]{1,0:T(8,128)(2,1)}) %all-gather.3.cloned.1.call-update) | async-done | bytes 1048592 | tf_op jit(solution)/shard_map/all_gather | solution.py:58
  50.9 1.5 fusion.17
  52.4 41.0 %all-gather.5.cloned.1.call-done = bf16[1024,1024]{1,0:T(8,128)(2,1)} async-done(((bf16[64,1024]{1,0:T(8,128)(2,1)}), bf16[1024,1024]{1,0:T(8,128)(2,1)}) %all-gather.5.cloned.1.call-update) | async-done | bytes 2097168 | tf_op jit(solution)/shard_map/all_gather | solution.py:59
  93.4 2.6 %multiply_reduce_fusion.1 = (f32[128]{0:T(128)S(1)}, f32[128,1024]{1,0:T(8,128)S(1)}) fusion(f32[1024]{0:T(1024)S(1)} %convert_element_type.33, bf16[1024,1024]{1,0:T(8,128)(2,1)} %all-gather.5.cloned.1.call-done, f32[128,1024]{1,0:T(8,128)S(1)} %fusion.17), kind=kOutput, calls=%fused_computation.16 | convolution fusion | flops 270401408 | bytes 3150336 | tf_op jit(solution)/shard_map/dot_general | solution.py:18
  96.7 1.7 multiply_convert_fusion.1
  98.9 1.1 multiply_convert_fusion
  100.0 0.9 add_reduce_fusion
  100.9 3.0 %fusion.2 = f32[1024,512]{1,0:T(8,128)S(1)} fusion(bf16[128,512]{1,0:T(8,128)(2,1)S(1)} %copy-done, bf16[128,1024]{1,0:T(8,128)(2,1)S(1)} %get-tuple-element.10, bf16[1024,1024]{1,0:T(8,128)(2,1)} %all-gather.5.cloned.1.call-done, f32[128,1024]{1,0:T(8,128)} %get-tuple-element.14, f32[128,1024]{1,0:T(8,128)} %get-tuple-element.12, f32[128,1024]{1,0:T(8,128)S(1)} %fusion.17), kind=kOutput, calls=%fused_computation.7 | convolution fusion | flops 403963904 | bytes 6160384 | tf_op jit(solution)/shard_map/dot_general | solution.py:8
  103.9 1.8 bitcast_add_fusion
  105.7 2.9 %copy.20 = f32[512,1024]{1,0:T(8,128)} copy(f32[512,1024]{0,1:T(8,128)} %bitcast_add_fusion) | data formatting | bytes 4194304
  108.7 1.0 copy-done.4
  109.7 0.8 fusion.11
  110.5 2.8 %convolution_add_fusion = f32[1024,1024]{1,0:T(8,128)} fusion(f32[1024,1024]{1,0:T(8,128)S(1)} %fusion.11, bf16[128,1024]{1,0:T(8,128)(2,1)S(1)} %get-tuple-element.10, f32[128,1024]{1,0:T(8,128)S(1)} %fusion.17), kind=kOutput, calls=%fused_computation | convolution fusion | flops 270401536 | bytes 9175040 | tf_op jit(solution)/shard_map/dot_general | solution.py:8
  113.3 0.9 copy-done.9
  114.4 31.6 %psum.7 = f32[1024]{0:T(1024)S(1)} all-reduce(f32[1024]{0:T(1024)S(1)} %get-tuple-element.9), channel_id=1, replica_groups=mesh['groups'=2,'blk'=16] {'blk'}, use_global_device_ids=true, to_apply=%region_7.8 | all-reduce | flops 1024 | bytes 8192 | tf_op jit(solution)/shard_map/psum | solution.py:80
  148.0 21.5 %reduce-scatter.7.cloned.1.call-done = f32[32,1024]{1,0:T(8,128)} async-done(((f32[512,1024]{1,0:T(8,128)}), f32[32,1024]{1,0:T(8,128)}) %reduce-scatter.7.cloned.1.call-update) | async-done | bytes 131088
  169.5 1.1 copy.21
  170.9 0.8 copy.18
  171.7 73.3 %reduce-scatter.5.cloned.1.call-done = f32[64,1024]{1,0:T(8,128)} async-done(((f32[1024,1024]{1,0:T(8,128)}), f32[64,1024]{1,0:T(8,128)}) %reduce-scatter.5.cloned.1.call-update) | async-done | bytes 262160 | tf_op jit(solution)/shard_map/reduce_scatter | solution.py:74
  245.0 1.1 multiply_reduce_fusion.2
  246.1 1.8 multiply_add_fusion.1
  (39 shorter events, 4.5 us)
Async XLA Ops:
  7.2 43.7 %copy-start = (bf16[128,512]{1,0:T(8,128)(2,1)S(1)}, bf16[128,512]{1,0:T(8,128)(2,1)}, u32[]{:S(2)}) copy-start(bf16[128,512]{1,0:T(8,128)(2,1)} %param.10) | copy-start | bytes 393220
  7.2 43.7 %all-gather.3.cloned.1.call-start = ((), (), s32[]{:S(2)}) async-start(), calls=%async_computation.2 | async-start | bytes 1114112 | tf_op jit(solution)/shard_map/all_gather | solution.py:58
  7.9 85.4 %all-gather.5.cloned.1.call-start = ((), (), s32[]{:S(2)}) async-start(), calls=%async_computation.3 | async-start | bytes 2228224 | tf_op jit(solution)/shard_map/all_gather | solution.py:59
  8.7 160.8 %reduce-scatter.7.cloned.1.call-start = ((), (), s32[]{:S(2)}) async-start(), calls=%async_computation.5 | async-start | bytes 2228224
  52.4 43.6 %copy-start.11 = (bf16[128]{0:T(256)(128)(2,1)S(1)}, bf16[128]{0:T(256)(128)(2,1)}, u32[]{:S(2)}) copy-start(bf16[128]{0:T(256)(128)(2,1)} %param.12) | copy-start | bytes 772
  93.4 3.3 %copy-start.2 = (bf16[1024,1024]{1,0:T(8,128)(2,1)S(1)}, bf16[1024,1024]{1,0:T(8,128)(2,1)}, u32[]{:S(2)}) copy-start(bf16[1024,1024]{1,0:T(8,128)(2,1)} %all-gather.5.cloned.1.call-done) | copy-start | bytes 6291460
  96.0 4.0 %copy-start.3 = (f32[128,1024]{1,0:T(8,128)}, f32[128,1024]{1,0:T(8,128)S(1)}, u32[]{:S(2)}) copy-start(f32[128,1024]{1,0:T(8,128)S(1)} %get-tuple-element.16) | copy-start | bytes 1572868
  96.7 1.7 copy-start.1
  96.7 1.7 copy-start.8
  100.0 0.9 copy-start.5
  108.6 1.0 copy-start.4
  108.6 1.1 copy-start.6
  108.7 136.4 %reduce-scatter.5.cloned.1.call-start = ((), (), s32[]{:S(2)}) async-start(), calls=%async_computation.4 | async-start | bytes 4456448 | tf_op jit(solution)/shard_map/reduce_scatter | solution.py:74
  113.3 0.9 copy-start.9
  113.3 34.0 %copy-start.10 = (f32[1024]{0:T(1024)S(1)}, f32[1024]{0:T(1024)}, u32[]{:S(2)}) copy-start(f32[1024]{0:T(1024)} %param.19) | copy-start | bytes 12292
  114.2 131.9 %copy-start.7 = (f32[64,1024]{1,0:T(8,128)S(1)}, f32[64,1024]{1,0:T(8,128)}, u32[]{:S(2)}) copy-start(f32[64,1024]{1,0:T(8,128)} %param.18) | copy-start | bytes 786436
Sparse Core Ops, SparseCore 0:
  10.2 40.6 all-gather.2
  53.0 40.3 all-gather.4
  108.8 60.6 reduce-scatter.6
  173.7 71.2 reduce-scatter.4
where the time goes:
time: 255 us; the launch traced here: 254 us
  waiting for transfers between devices  177 us (69%)
  blocking collectives  31.6 us (12%)
  matrix products  16.7 us (7%)
  between operations  14.6 us (6%)
  other arithmetic  7.63 us (3%)
  local copies, waits for them, and re-layouts  6.99 us (3%)
    reduce_scatter x1, waiting for transfers between devices, per_device(): lax.psum_scatter(rows_product(e_cone, g_two) + rows_product(h_one, e_atwo...  73.3 us
    all_gather x1, waiting for transfers between devices, per_device(): lax.all_gather(w_second, 'blk', axis=0, tiled=True)  41 us
    all_gather x1, waiting for transfers between devices, per_device(): lax.all_gather(w_first, 'blk', axis=0, tiled=True)  39.5 us
    psum x1, blocking collectives, per_device(): grad_out = lax.psum(grad_three, 'blk')  31.6 us
    unnamed x5, waiting for transfers between devices  22.9 us
    dot_general x4, matrix products, rows_product(): lax.dot_general(left, right, (((0,), (0,)), ((), ())), preferred_element_...  8.39 us
    unnamed x28, local copies, waits for them, and re-layouts  6.99 us
  transfers between devices with their start and end apart: 4, of which 4 were waited for; matrix products, arithmetic and copies ran while one was open for 4% of the time, Pallas kernels for 0%

commit v1 on v0

--- a/solution.py
+++ b/solution.py
@@ -2,6 +2,25 @@
 import jax.numpy as jnp
 from jax import lax
 from jax.sharding import PartitionSpec as P
+
+
+def patches_watch(local_x, ndim_at):
+    w_next = list(local_x.shape[1:])
+    w_next[ndim_at] *= local_x.shape[0]
+    return jnp.moveaxis(local_x, 0, ndim_at).reshape(w_next)
+
+
+def fields_process(state, device_axis):
+    wide_n = lax.psum(1, device_axis)
+    t1 = state[None]
+    for d in range(wide_n.bit_length() - 1):
+        w2 = 1 << d
+        b_now = lax.ppermute(t1, device_axis, [(u, u ^ w2) for u in range(wide_n)])
+        last = jnp.stack([t1, b_now], 0)
+        tmp = lax.axis_index(device_axis)
+        upper = tmp >> d & 1
+        t1 = jnp.where(upper == 0, last, last[::-1]).reshape(-1, *state.shape)
+    return t1
 
 
 def rows_product(left, right):
@@ -52,10 +71,15 @@
 def per_device(
     paths, deltas, payoffs, counts, w_first, w_second, w_out, mom_first, mom_second, mom_out
 ):
+
+    def update_bench(here_x, d0, own_rows):
+        state_now = fields_process(own_rows, here_x)
+        return patches_watch(state_now, d0)
+
     position = lax.axis_index("blk")
     rows_dev = paths.shape[0]
     w_one, w_two = (
-        lax.all_gather(w_first, "blk", axis=0, tiled=True),
+        update_bench("blk", 0, own_rows=w_first),
         lax.all_gather(w_second, "blk", axis=0, tiled=True),
     )
     sending = lax.dynamic_index_in_dim(counts, position, 0, keepdims=False)

time: 255 us -> 228 us (0.89)
  waiting for transfers between devices: 177 us -> 141 us
  starting transfers between devices: 0.16 us -> 8.15 us
    all_gather x1 -> x0, waiting for transfers between devices: 39.5 us -> none  [per_device(): lax.all_gather(w_first, 'blk', axis=0, tiled=True)]
    ppermute x0 -> x4, waiting for transfers between devices: none -> 38.3 us  [fields_process(): b_now = lax.ppermute(t1, device_axis, [(u, u ^ w2) for u in range(wide_n)])]
    all_gather x1, waiting for transfers between devices: 41 us -> 7.28 us  [per_device(): lax.all_gather(w_second, 'blk', axis=0, tiled=True)]
    ppermute x0 -> x4, starting transfers between devices: none -> 8.03 us  [fields_process(): b_now = lax.ppermute(t1, device_axis, [(u, u ^ w2) for u in range(wide_n)])]
    unnamed x5 -> x4, waiting for transfers between devices: 22.9 us -> 22.2 us
  transfers between devices with their start and end apart: 4 -> 7, of which waited for: 4 -> 7; matrix products, arithmetic and copies ran while one was open for 4% -> 5% of each run, Pallas kernels for 0% -> 0%
where the time goes in v1:
time: 228 us
  waiting for transfers between devices  141 us (62%)
  blocking collectives  31.9 us (14%)
  matrix products  16.7 us (7%)
  between operations  14.7 us (6%)
  other arithmetic  8.39 us (4%)
  starting transfers between devices  8.15 us (4%)
  local copies, waits for them, and re-layouts  6.98 us (3%)
    reduce_scatter x1, waiting for transfers between devices, per_device(): lax.psum_scatter(rows_product(e_cone, g_two) + rows_product(h_one, e_atwo...  73.5 us
    ppermute x4, waiting for transfers between devices, fields_process(): b_now = lax.ppermute(t1, device_axis, [(u, u ^ w2) for u in range(wide_n)])  38.3 us
    psum x1, blocking collectives, per_device(): grad_out = lax.psum(grad_three, 'blk')  31.9 us
    unnamed x4, waiting for transfers between devices  22.2 us
    dot_general x4, matrix products, rows_product(): lax.dot_general(left, right, (((0,), (0,)), ((), ())), preferred_element_...  8.47 us
    ppermute x4, starting transfers between devices, fields_process(): b_now = lax.ppermute(t1, device_axis, [(u, u ^ w2) for u in range(wide_n)])  8.03 us
    all_gather x1, waiting for transfers between devices, per_device(): lax.all_gather(w_second, 'blk', axis=0, tiled=True)  7.28 us
    unnamed x28, local copies, waits for them, and re-layouts  6.98 us
  transfers between devices with their start and end apart: 7, of which 7 were waited for; matrix products, arithmetic and copies ran while one was open for 5% of the time, Pallas kernels for 0%

profile of v1, /device:TPU:0, one launch (start us, length us, event | category | flops | bytes accessed | tf_op | source)
XLA Modules:
  0.0 228.1 jit_solution(1540560880228306558)
XLA Ops:
  8.5 1.1 collective-permute-done
  10.5 2.9 %collective-permute-start.1 = (bf16[2,32,1024]{2,1,0:T(8,128)(2,1)S(1)}, bf16[2,32,1024]{2,1,0:T(8,128)(2,1)S(1)}, u32[]{:S(2)}, u32[]{:S(2)}) collective-permute-start(bf16[2,32,1024]{2,1,0:T(8,128)(2,1)S(1)} %get-tuple-element.12), channel_id=1, source_target_pairs={{0,2},{1,3},{2,0},{3,1},{4,6},{5,7},{6,4},{7,5},{8,10},{9,11},{10,... | collective-permute-start | bytes 393224 | tf_op jit(solution)/shard_map/ppermute | solution.py:18
  13.4 3.8 %collective-permute-done.1 = bf16[2,32,1024]{2,1,0:T(8,128)(2,1)S(1)} collective-permute-done((bf16[2,32,1024]{2,1,0:T(8,128)(2,1)S(1)}, bf16[2,32,1024]{2,1,0:T(8,128)(2,1)S(1)}, u32[]{:S(2)}, u32[]{:S(2)}) %collective-permute-start.1) | collective-permute-done | bytes 131104 | tf_op jit(solution)/shard_map/ppermute | solution.py:18
  17.3 1.9 collective-permute-start.2
  19.2 7.5 %collective-permute-done.2 = bf16[4,32,1024]{2,1,0:T(8,128)(2,1)S(1)} collective-permute-done((bf16[4,32,1024]{2,1,0:T(8,128)(2,1)S(1)}, bf16[4,32,1024]{2,1,0:T(8,128)(2,1)S(1)}, u32[]{:S(2)}, u32[]{:S(2)}) %collective-permute-start.2) | collective-permute-done | bytes 262176 | tf_op jit(solution)/shard_map/ppermute | solution.py:18
  26.8 2.7 %collective-permute-start.3 = (bf16[8,32,1024]{2,1,0:T(8,128)(2,1)S(1)}, bf16[8,32,1024]{2,1,0:T(8,128)(2,1)S(1)}, u32[]{:S(2)}, u32[]{:S(2)}) collective-permute-start(bf16[8,32,1024]{2,1,0:T(8,128)(2,1)S(1)} %bitcast.40), channel_id=1, source_target_pairs={{0,8},{1,9},{2,10},{3,11},{4,12},{5,13},{6,14},{7,15},{8,0},{9,1},... | collective-permute-start | bytes 1572872 | tf_op jit(solution)/shard_map/ppermute | solution.py:18
  29.6 1.3 dynamic-slice_reduce_fusion
  31.5 25.9 %collective-permute-done.3 = bf16[8,32,1024]{2,1,0:T(8,128)(2,1)S(1)} collective-permute-done((bf16[8,32,1024]{2,1,0:T(8,128)(2,1)S(1)}, bf16[8,32,1024]{2,1,0:T(8,128)(2,1)S(1)}, u32[]{:S(2)}, u32[]{:S(2)}) %collective-permute-start.3) | collective-permute-done | bytes 524320 | tf_op jit(solution)/shard_map/ppermute | solution.py:18
  58.3 7.3 %all-gather.2.cloned.1.call-done = bf16[1024,1024]{1,0:T(8,128)(2,1)} async-done(((bf16[64,1024]{1,0:T(8,128)(2,1)}), bf16[1024,1024]{1,0:T(8,128)(2,1)}) %all-gather.2.cloned.1.call-update) | async-done | bytes 2097168 | tf_op jit(solution)/shard_map/all_gather | solution.py:83
  65.6 2.9 %multiply_reduce_fusion.1 = (f32[128]{0:T(128)S(1)}, f32[128,1024]{0,1:T(8,128)S(1)}) fusion(f32[1024]{0:T(1024)S(1)} %convert_element_type.33, bf16[1024,1024]{1,0:T(8,128)(2,1)} %all-gather.2.cloned.1.call-done, f32[128,1024]{0,1:T(8,128)S(1)} %convolution_bitcast_fusion), kind=kOutput, calls=%fused_computation.21 | convolution fusion | flops 270401408 | bytes 3150336 | tf_op jit(solution)/shard_map/dot_general | solution.py:37
  68.5 1.6 multiply_convert_fusion.1
  70.7 1.3 multiply_convert_fusion
  72.7 1.4 add_reduce_fusion
  74.1 3.2 %fusion.2 = f32[1024,512]{1,0:T(8,128)S(1)} fusion(bf16[128,512]{1,0:T(8,128)(2,1)S(1)} %copy-done, bf16[1024,1024]{1,0:T(8,128)(2,1)} %all-gather.2.cloned.1.call-done, bf16[128,1024]{0,1:T(8,128)(2,1)S(1)} %get-tuple-element.10, f32[128,1024]{0,1:T(8,128)} %get-tuple-element.16, f32[128,1024]{0,1:T(8,128)} %get-tuple-element.14, ...), kind=kOutput, calls=%fused_computation.9 | convolution fusion | flops 403963904 | bytes 6160384 | tf_op jit(solution)/shard_map/dot_general | solution.py:27
  77.2 1.8 bitcast_add_fusion
  79.0 2.9 %copy.48 = f32[512,1024]{1,0:T(8,128)} copy(f32[512,1024]{0,1:T(8,128)} %bitcast_add_fusion) | data formatting | bytes 4194304
  82.0 1.0 copy-done.3
  83.8 2.7 %convolution_add_fusion = f32[1024,1024]{1,0:T(8,128)} fusion(f32[1024,1024]{1,0:T(8,128)S(1)} %fusion.17, bf16[128,1024]{0,1:T(8,128)(2,1)S(1)} %get-tuple-element.10, f32[128,1024]{0,1:T(8,128)S(1)} %convolution_bitcast_fusion), kind=kOutput, calls=%fused_computation | convolution fusion | flops 270401536 | bytes 9175040 | tf_op jit(solution)/shard_map/dot_general | solution.py:27
  87.7 31.9 %psum.7 = f32[1024]{0:T(1024)S(1)} all-reduce(f32[1024]{0:T(1024)S(1)} %get-tuple-element.9), channel_id=1, replica_groups=mesh['groups'=2,'blk'=16] {'blk'}, use_global_device_ids=true, to_apply=%region_7.8 | all-reduce | flops 1024 | bytes 8192 | tf_op jit(solution)/shard_map/psum | solution.py:104
  121.5 21.5 %reduce-scatter.7.cloned.1.call-done = f32[32,1024]{1,0:T(8,128)} async-done(((f32[512,1024]{1,0:T(8,128)}), f32[32,1024]{1,0:T(8,128)}) %reduce-scatter.7.cloned.1.call-update) | async-done | bytes 131088
  142.9 1.1 copy.49
  145.1 73.5 %reduce-scatter.5.cloned.1.call-done = f32[64,1024]{1,0:T(8,128)} async-done(((f32[1024,1024]{1,0:T(8,128)}), f32[64,1024]{1,0:T(8,128)}) %reduce-scatter.5.cloned.1.call-update) | async-done | bytes 262160 | tf_op jit(solution)/shard_map/reduce_scatter | solution.py:98
  218.7 1.1 multiply_reduce_fusion.2
  219.8 1.8 multiply_add_fusion.1
  (52 shorter events, 9.4 us)
Async XLA Ops:
  7.2 50.7 %copy-start = (bf16[128,512]{1,0:T(8,128)(2,1)S(1)}, bf16[128,512]{1,0:T(8,128)(2,1)}, u32[]{:S(2)}) copy-start(bf16[128,512]{1,0:T(8,128)(2,1)} %param.10) | copy-start | bytes 393220
  7.2 22.4 %copy-start.10 = (bf16[1024]{0:T(1024)(128)(2,1)S(1)}, bf16[1024]{0:T(1024)(128)(2,1)}, u32[]{:S(2)}) copy-start(bf16[1024]{0:T(1024)(128)(2,1)} %param.16) | copy-start | bytes 6148
  7.2 58.4 %all-gather.2.cloned.1.call-start = ((), (), s32[]{:S(2)}) async-start(), calls=%async_computation.2 | async-start | bytes 2228224 | tf_op jit(solution)/shard_map/all_gather | solution.py:83
  7.9 135.0 %reduce-scatter.7.cloned.1.call-start = ((), (), s32[]{:S(2)}) async-start(), calls=%async_computation.4 | async-start | bytes 2228224
  8.0 1.6 collective-permute-start
  10.5 6.8 %collective-permute-start.1 = (bf16[2,32,1024]{2,1,0:T(8,128)(2,1)S(1)}, bf16[2,32,1024]{2,1,0:T(8,128)(2,1)S(1)}, u32[]{:S(2)}, u32[]{:S(2)}) collective-permute-start(bf16[2,32,1024]{2,1,0:T(8,128)(2,1)S(1)} %get-tuple-element.12), channel_id=1, source_target_pairs={{0,2},{1,3},{2,0},{3,1},{4,6},{5,7},{6,4},{7,5},{8,10},{9,11},{10,... | collective-permute-start | bytes 393224 | tf_op jit(solution)/shard_map/ppermute | solution.py:18
  17.3 9.3 %collective-permute-start.2 = (bf16[4,32,1024]{2,1,0:T(8,128)(2,1)S(1)}, bf16[4,32,1024]{2,1,0:T(8,128)(2,1)S(1)}, u32[]{:S(2)}, u32[]{:S(2)}) collective-permute-start(bf16[4,32,1024]{2,1,0:T(8,128)(2,1)S(1)} %bitcast.42), channel_id=1, source_target_pairs={{0,4},{1,5},{2,6},{3,7},{4,0},{5,1},{6,2},{7,3},{8,12},{9,13},{10,... | collective-permute-start | bytes 786440 | tf_op jit(solution)/shard_map/ppermute | solution.py:18
  26.8 30.7 %collective-permute-start.3 = (bf16[8,32,1024]{2,1,0:T(8,128)(2,1)S(1)}, bf16[8,32,1024]{2,1,0:T(8,128)(2,1)S(1)}, u32[]{:S(2)}, u32[]{:S(2)}) collective-permute-start(bf16[8,32,1024]{2,1,0:T(8,128)(2,1)S(1)} %bitcast.40), channel_id=1, source_target_pairs={{0,8},{1,9},{2,10},{3,11},{4,12},{5,13},{6,14},{7,15},{8,0},{9,1},... | collective-permute-start | bytes 1572872 | tf_op jit(solution)/shard_map/ppermute | solution.py:18
  65.6 2.9 %copy-start.1 = (bf16[1024,1024]{1,0:T(8,128)(2,1)S(1)}, bf16[1024,1024]{1,0:T(8,128)(2,1)}, u32[]{:S(2)}) copy-start(bf16[1024,1024]{1,0:T(8,128)(2,1)} %all-gather.2.cloned.1.call-done) | copy-start | bytes 6291460
  68.5 4.2 %copy-start.2 = (f32[128,1024]{0,1:T(8,128)}, f32[128,1024]{0,1:T(8,128)S(1)}, u32[]{:S(2)}) copy-start(f32[128,1024]{0,1:T(8,128)S(1)} %get-tuple-element.18) | copy-start | bytes 1572868
  68.5 1.7 copy-start.7
  70.2 1.8 copy-start.11
  72.0 2.0 copy-start.4
  81.9 1.0 copy-start.3
  81.9 1.1 copy-start.5
  81.9 136.8 %reduce-scatter.5.cloned.1.call-start = ((), (), s32[]{:S(2)}) async-start(), calls=%async_computation.3 | async-start | bytes 4456448 | tf_op jit(solution)/shard_map/reduce_scatter | solution.py:98
  86.6 0.9 copy-start.8
  86.6 34.3 %copy-start.9 = (f32[1024]{0:T(1024)S(1)}, f32[1024]{0:T(1024)}, u32[]{:S(2)}) copy-start(f32[1024]{0:T(1024)} %param.19) | copy-start | bytes 12292
  87.5 132.3 %copy-start.6 = (f32[64,1024]{1,0:T(8,128)S(1)}, f32[64,1024]{1,0:T(8,128)}, u32[]{:S(2)}) copy-start(f32[64,1024]{1,0:T(8,128)} %param.18) | copy-start | bytes 786436
Sparse Core Ops, SparseCore 0:
  10.2 55.3 all-gather.1
  82.1 60.8 reduce-scatter.6
  147.3 71.3 reduce-scatter.4
